TPU v7x, 256 devices: a whole 4x4x8 slice. The times are simulated.
256 devices in a mesh: req: 32 (over z, y_hi, core), tp: 8 (over x, y_lo).
Axes of the slice: x: 4, y: 4 (y_hi: 2, y_lo: 2; y = y_hi * 2 + y_lo), z: 8, core: 2. Of those that a mesh axis runs over, the one named last changes fastest.
Arguments:
- tokens: bfloat16 [16384, 1024], P(('req', 'tp')), may hold values from -6 to 6
- w_qkv: bfloat16 [1024, 3, 1024], P(None, None, 'tp'), may hold values from -0.1875 to 0.1875
- w_out: bfloat16 [1024, 1024], P('tp'), may hold values from -0.75 to 0.75
- w_up: bfloat16 [1024, 4096], P(None, 'tp'), may hold values from -0.1875 to 0.1875
- b_up: float32 [4096], P('tp'), may hold values from -4 to 4
- w_down: bfloat16 [4096, 1024], P('tp'), may hold values from -0.09375 to 0.09375
- b_down: float32 [1024], replicated, may hold values from -3 to 3
- ln1_gain: float32 [1024], replicated, may hold values from 0.5 to 1.5
- ln1_bias: float32 [1024], replicated, may hold values from -3 to 3
- ln2_gain: float32 [1024], replicated, may hold values from 0.5 to 1.5
- ln2_bias: float32 [1024], replicated, may hold values from -3 to 3
- kv_cache: bfloat16 [2, 32, 16384, 1024], P(None, None, 'req', 'tp'), may hold values from -122 to 122
- cache_len: int32 [32], replicated, may hold values from 0 to 16384, as said below
- span_len: int32 [32], replicated, may hold values from 1 to 512, as said below
Outputs:
- output: bfloat16 [16384, 1024], P(('req', 'tp'))
Inputs may be any that keep to these rules, and one draw needn't show every extreme that they name: The first cache_len[r] positions of request r hold its keys and values; some request has 16384. Slots from span_len[r] on are padding whose keys are not attended to; some request has 512.
All inputs are finite; a program needn't handle non-finite values.
Results may differ from a plain program's by a relative error of at most 0.015.
Values may be sent and summed in bfloat16 or wider, within the bound.
No kernel may reach another device: no remote copies, remote signals or barrier semaphores. Data moves between devices by JAX's collectives and lax.ppermute only.
A program may use at most 128 MiB of HBM per device.

v0:
```python
import jax
import jax.numpy as jnp
from jax import lax
from jax.experimental import pallas as pl
from jax.experimental.pallas import tpu as pltpu
from jax.sharding import PartitionSpec as P

HEAD_DIM = 64
BLEND_STEP = 4

masked_score = -1e30


def layer_norm(values, gain, bias):
    centre = jnp.mean(values, axis=-1, keepdims=True)
    centred = values - centre
    variance = jnp.mean(centred * centred, axis=-1, keepdims=True)
    return centred * lax.rsqrt(variance + 1e-05) * gain + bias


def partial_attention(queries, key_rows, value_rows, allowed):
    scores = jnp.einsum(
        "chd,nhd->hcn", queries, key_rows, preferred_element_type=jnp.float32
    ) * queries.shape[-1] ** (-0.5)
    scores = jnp.where(allowed[None], scores, masked_score)
    peaks = jnp.max(scores, axis=-1)
    weights = jnp.where(allowed[None], jnp.exp(scores - peaks[..., None]), 0.0).astype(jnp.bfloat16)
    weight_sums = jnp.sum(weights.astype(jnp.float32), axis=-1)
    blended = jnp.einsum("hcn,nhd->chd", weights, value_rows, preferred_element_type=jnp.float32)
    return (peaks.T, weight_sums.T, blended.reshape(blended.shape[0], -1))


def merge_axis(peaks, weight_sums, blended, axis):
    highest = jnp.max(peaks, axis=axis, keepdims=True)
    factors = jnp.exp(peaks - highest)
    sums_out = jnp.sum(factors * weight_sums, axis=axis)
    spread = jnp.repeat(factors, blended.shape[-1] // peaks.shape[-1], axis=-1)
    blend_out = jnp.sum(spread * blended, axis=axis)
    return (jnp.squeeze(highest, axis=axis), sums_out, blend_out)


def score_kernel(count_ref, qt_ref, k_ref, w_ref, peak_ref):
    block = pl.program_id(0)
    heads = qt_ref.shape[0]
    width = k_ref.shape[1]
    start = block * width
    scale = HEAD_DIM ** (-0.5)

    def step(masked):
        allowed = start + lax.broadcasted_iota(jnp.int32, (width, 1), 0) < count_ref[0]
        for head in range(heads):
            raw = jnp.dot(k_ref[0], qt_ref[head], preferred_element_type=jnp.float32)
            if masked:
                raw = jnp.where(allowed, raw, masked_score)
            top = jnp.max(raw, axis=0, keepdims=True)
            weights = jnp.exp((raw - top) * scale)
            if masked:
                weights = jnp.where(allowed, weights, 0.0)
            w_ref[0, head] = weights.astype(jnp.bfloat16)
            peak_ref[0, head] = top * scale

    full = start + width <= count_ref[0]
    some = start < count_ref[0]

    @pl.when(full)
    def _():
        step(False)

    @pl.when(some & jnp.logical_not(full))
    def _():
        step(True)

    @pl.when(jnp.logical_not(some))
    def _():
        w_ref[...] = jnp.zeros_like(w_ref)
        peak_ref[...] = jnp.full_like(peak_ref, masked_score)


def blend_kernel(count_ref, w_ref, block_peak_ref, vt_ref, acc_ref, peak_ref):
    step = pl.program_id(0)
    per_step, heads = w_ref.shape[0], w_ref.shape[1]
    width = vt_ref.shape[2]

    @pl.when(step == 0)
    def _():
        acc_ref[...] = jnp.zeros_like(acc_ref)
        peak_ref[...] = jnp.full_like(peak_ref, masked_score)

    for sub in range(per_step):
        start = (step * per_step + sub) * width

        @pl.when(start < count_ref[0])
        def _():
            row = lax.broadcasted_iota(jnp.int32, (vt_ref.shape[1], 1), 0)
            for head in range(heads):
                own = (row >= head * HEAD_DIM) & (row < (head + 1) * HEAD_DIM)
                values = jnp.where(own, vt_ref[sub], jnp.ones_like(vt_ref[sub]))
                blend = jnp.dot(values, w_ref[sub, head], preferred_element_type=jnp.float32)
                peak = block_peak_ref[sub, head]
                old = peak_ref[head]
                new = jnp.maximum(old, peak)
                peak_ref[head] = new
                acc_ref[head] = acc_ref[head] * jnp.exp(old - new) + blend * jnp.exp(peak - new)


def block_weights(queries, own_keys, cached_count):
    span, width = queries.shape
    total_blocks, block_width = own_keys.shape[0], own_keys.shape[1]
    heads = width // HEAD_DIM
    row = jnp.arange(width)[None, :, None] // HEAD_DIM
    padded = jnp.where(row == jnp.arange(heads)[:, None, None], queries.T[None], jnp.zeros_like(queries.T)[None])
    grid_spec = pltpu.PrefetchScalarGridSpec(
        num_scalar_prefetch=1,
        grid=(total_blocks,),
        in_specs=[
            pl.BlockSpec((heads, width, span), lambda b, c: (0, 0, 0)),
            pl.BlockSpec((1, block_width, width), lambda b, c: (b, 0, 0)),
        ],
        out_specs=[
            pl.BlockSpec((1, heads, block_width, span), lambda b, c: (b, 0, 0, 0)),
            pl.BlockSpec((1, heads, 1, span), lambda b, c: (b, 0, 0, 0)),
        ],
    )
    return pl.pallas_call(
        score_kernel,
        grid_spec=grid_spec,
        out_shape=[
            jax.ShapeDtypeStruct((total_blocks, heads, block_width, span), jnp.bfloat16),
            jax.ShapeDtypeStruct((total_blocks, heads, 1, span), jnp.float32),
        ],
        compiler_params=pltpu.CompilerParams(dimension_semantics=("arbitrary",)),
        cost_estimate=pl.CostEstimate(
            flops=2 * span * block_width * width * heads * total_blocks,
            transcendentals=heads * span * block_width * total_blocks,
            bytes_accessed=own_keys.size * 2 + total_blocks * heads * span * block_width * 2,
        ),
    )(jnp.reshape(cached_count, (1,)), padded, own_keys)


def cache_partials(weights, block_peaks, own_value_rows, cached_count):
    total_blocks, heads, block_width, span = weights.shape
    width = own_value_rows.shape[1]
    per_step = BLEND_STEP if total_blocks % BLEND_STEP == 0 else 1
    grid_spec = pltpu.PrefetchScalarGridSpec(
        num_scalar_prefetch=1,
        grid=(total_blocks // per_step,),
        in_specs=[
            pl.BlockSpec((per_step, heads, block_width, span), lambda b, c: (b, 0, 0, 0)),
            pl.BlockSpec((per_step, heads, 1, span), lambda b, c: (b, 0, 0, 0)),
            pl.BlockSpec((per_step, width, block_width), lambda b, c: (b, 0, 0)),
        ],
        out_specs=[
            pl.BlockSpec((heads, width, span), lambda b, c: (0, 0, 0)),
            pl.BlockSpec((heads, 1, span), lambda b, c: (0, 0, 0)),
        ],
    )
    acc, peaks = pl.pallas_call(
        blend_kernel,
        grid_spec=grid_spec,
        out_shape=[
            jax.ShapeDtypeStruct((heads, width, span), jnp.float32),
            jax.ShapeDtypeStruct((heads, 1, span), jnp.float32),
        ],
        compiler_params=pltpu.CompilerParams(dimension_semantics=("arbitrary",)),
        cost_estimate=pl.CostEstimate(
            flops=2 * span * block_width * width * heads * total_blocks,
            transcendentals=2 * heads * span * total_blocks,
            bytes_accessed=weights.size * 2 + own_value_rows.size * 2 + heads * span * width * 4,
        ),
    )(jnp.reshape(cached_count, (1,)), weights, block_peaks, own_value_rows)
    spare = [((head + 1) % heads) * HEAD_DIM for head in range(heads)]
    blended = jnp.concatenate([acc[head, head * HEAD_DIM : (head + 1) * HEAD_DIM, :] for head in range(heads)], axis=0).T
    sums = jnp.stack([acc[head, spare[head], :] for head in range(heads)], axis=1)
    return peaks[:, 0, :].T, sums, blended


def shards(
    tokens,
    w_qkv,
    w_out,
    w_up,
    b_up,
    w_down,
    b_down,
    ln1_gain,
    ln1_bias,
    ln2_gain,
    ln2_bias,
    kv_cache,
    cache_len,
    span_len,
):
    width_here = w_qkv.shape[2]
    heads_here = width_here // HEAD_DIM
    where_req = lax.axis_index("req")

    own_keys = lax.all_to_all(kv_cache[0], "req", split_axis=0, concat_axis=0, tiled=True)
    own_keys, value_rows = lax.optimization_barrier((own_keys, jnp.swapaxes(kv_cache[1], 1, 2)))
    own_value_rows = lax.all_to_all(value_rows, "req", split_axis=0, concat_axis=0, tiled=True)

    span_rows = lax.all_gather(tokens, "tp", axis=0, tiled=True)
    flat_qkv = w_qkv.reshape(w_qkv.shape[0], 3 * width_here)
    heads_qkv = jnp.dot(span_rows, flat_qkv, preferred_element_type=jnp.float32).astype(jnp.bfloat16)
    span = heads_qkv.shape[0]
    local_shape = (span, heads_here, HEAD_DIM)
    queries = heads_qkv[:, :width_here].reshape(local_shape)
    fresh_keys = heads_qkv[:, width_here : 2 * width_here].reshape(local_shape)
    fresh_values = heads_qkv[:, 2 * width_here :].reshape(local_shape)

    full_out = lax.all_gather(w_out, "tp", axis=0, tiled=True)

    fresh_count = span_len[where_req]
    cached_count = cache_len[where_req]
    positions = jnp.arange(span, dtype=jnp.int32)
    allowed = (positions[None, :] <= positions[:, None]) & (positions[None, :] < fresh_count)
    fresh = partial_attention(queries, fresh_keys, fresh_values, allowed)

    weights, block_peaks = block_weights(heads_qkv[:, :width_here], own_keys, cached_count)
    peaks, weight_sums, blended = cache_partials(weights, block_peaks, own_value_rows, cached_count)
    peaks, weight_sums, blended = merge_axis(
        jnp.stack([fresh[0], peaks]),
        jnp.stack([fresh[1], weight_sums]),
        jnp.stack([fresh[2], blended]),
        0,
    )
    attention = (blended / jnp.repeat(weight_sums, HEAD_DIM, axis=-1)).astype(jnp.bfloat16)
    attention = lax.all_to_all(attention, "tp", split_axis=0, concat_axis=1, tiled=True)

    projected = jnp.dot(attention, full_out, preferred_element_type=jnp.float32)
    normed = layer_norm(tokens.astype(jnp.float32) + projected, ln1_gain, ln1_bias).astype(jnp.bfloat16)
    n_tp = lax.axis_size("tp")
    span_normed = lax.all_to_all(
        jnp.broadcast_to(normed[None], (n_tp,) + normed.shape), "tp", split_axis=0, concat_axis=0, tiled=True
    ).reshape(-1, normed.shape[1])
    hidden = jax.nn.gelu(
        jnp.dot(span_normed, w_up, preferred_element_type=jnp.float32) + b_up,
        approximate=False,
    ).astype(jnp.bfloat16)
    partial = jnp.dot(hidden, w_down, preferred_element_type=jnp.float32).astype(jnp.bfloat16)
    partial = lax.all_to_all(
        partial.reshape((n_tp, -1) + partial.shape[1:]), "tp", split_axis=0, concat_axis=0, tiled=True
    )
    summed = jnp.sum(partial.astype(jnp.float32), axis=0) + b_down + normed.astype(jnp.float32)
    return layer_norm(summed, ln2_gain, ln2_bias).astype(jnp.bfloat16)


def solution(mesh):
    placed = (
        P(("req", "tp"), None),
        P(None, None, "tp"),
        P("tp", None),
        P(None, "tp"),
        P("tp"),
        P("tp", None),
        P(),
        P(),
        P(),
        P(),
        P(),
        P(None, None, "req", "tp"),
        P(),
        P(),
    )
    return jax.shard_map(
        shards, mesh=mesh, in_specs=placed, out_specs=P(("req", "tp"), None), check_vma=False
    )
```

profile of v0, /device:TPU:80, one launch (start us, length us, event | category | flops | bytes accessed | tf_op | source)
XLA Modules:
  0.0 303.3 jit_solution(2222689999922785665)
XLA Ops:
  6.5 6.0 %fusion.80 = (bf16[1,32,512,128]{3,2,1,0:T(8,128)(2,1)}, bf16[32,512,128]{2,1,0:T(8,128)(2,1)}) fusion(bf16[2,32,512,128]{3,2,1,0:T(8,128)(2,1)} %param.25), kind=kLoop, calls=%fused_computation.128 | loop fusion | bytes 16777216 | tf_op jit(solution)/shard_map/slice | solution.py:198
  12.5 10.7 %all-to-all-start = ((bf16[32,512,128]{2,1,0:T(8,128)(2,1)}), bf16[32,512,128]{2,1,0:T(8,128)(2,1)}, u32[]{:S(2)}, u32[]{:S(2)}) async-start(bf16[32,512,128]{2,1,0:T(8,128)(2,1)} %get-tuple-element.20), calls=%async_computation | async-start | bytes 8388608 | tf_op jit(solution)/shard_map/all_to_all | solution.py:197
  23.3 6.5 %copy.28 = bf16[1,32,512,128]{2,3,1,0:T(8,128)(2,1)} copy(bf16[1,32,512,128]{3,2,1,0:T(8,128)(2,1)} %get-tuple-element.19) | data formatting | bytes 8388608
  29.8 88.2 %all-to-all-done.k_ref = bf16[32,512,128]{2,1,0:T(8,128)(2,1)} async-done(((bf16[32,512,128]{2,1,0:T(8,128)(2,1)}), bf16[32,512,128]{2,1,0:T(8,128)(2,1)}, u32[]{:S(2)}, u32[]{:S(2)}) %all-to-all-start) | async-done | bytes 4194336 | tf_op jit(solution)/shard_map/all_to_all | solution.py:197
  118.0 7.0 %all-to-all-start.1 = ((bf16[32,128,512]{2,1,0:T(8,128)(2,1)}), bf16[32,128,512]{2,1,0:T(8,128)(2,1)}, u32[]{:S(2)}, u32[]{:S(2)}) async-start(bf16[32,128,512]{2,1,0:T(8,128)(2,1)} %bitcast.68), calls=%async_computation.1 | async-start | bytes 8388608 | tf_op jit(solution)/shard_map/all_to_all | solution.py:199
  125.0 0.7 all-gather.3.cloned.1.call-update
  125.8 0.7 all-gather.5.cloned.1.call-update
  126.8 0.7 dynamic_slice.7.count_ref
  127.5 0.6 dynamic_slice.6
  128.1 0.6 iota_compare_fusion.1
  128.9 54.7 %all-gather.3.cloned.1.call-done = bf16[512,1024]{1,0:T(8,128)(2,1)} async-done(((bf16[64,1024]{1,0:T(8,128)(2,1)}), bf16[512,1024]{1,0:T(8,128)(2,1)}) %all-gather.3.cloned.1.call-update) | async-done | bytes 1048592 | tf_op jit(solution)/shard_map/all_gather | solution.py:201
  183.5 1.8 convolution_convert_fusion.1
  185.4 0.8 broadcast_select_fusion.qt_ref
  186.2 0.6 fusion
  186.8 0.8 convolution_bitcast_fusion
  187.6 0.6 convert_reduce_fusion.1
  188.2 28.7 %shard_map.136 = (bf16[32,2,512,512]{3,2,1,0:T(8,128)(2,1)}, f32[32,2,1,512]{3,2,1,0:T(1,128)}) custom-call(s32[1]{0:T(128)} %dynamic_slice.7.count_ref, bf16[2,128,512]{2,1,0:T(8,128)(2,1)} %broadcast_select_fusion.qt_ref, bf16[32,512,128]{2,1,0:T(8,128)(2,1)} %all-to-all-done.k_ref), custom_call_target="tpu_custom_call" | custom-call | flops 4294967296 | bytes 37748736 | tf_op jit(solution)/shard_map/pallas_call | solution.py:124
  216.9 2.3 all-to-all-done.1.vt_ref
  219.2 15.5 %shard_map.137 = (f32[2,128,512]{2,1,0:T(8,128)}, f32[2,1,512]{2,1,0:T(1,128)}) custom-call(s32[1]{0:T(128)} %dynamic_slice.7.count_ref, bf16[32,2,512,512]{3,2,1,0:T(8,128)(2,1)} %get-tuple-element.12.w_ref, f32[32,2,1,512]{3,2,1,0:T(1,128)} %get-tuple-element.13.block_peak_ref, bf16[32,128,512]{2,1,0:T(8,128)(2,1)} %all-to-all-done.1.vt_ref), custom_call_target="tpu_custom_call" | custom-call | flops 4294967296 | bytes 38273024 | tf_op jit(solution)/shard_map/pallas_call | solution.py:157
  234.8 0.7 copy.38
  235.5 0.7 slice_bitcast_fusion.4
  236.2 1.0 slice_bitcast_fusion.2
  237.3 0.7 bitcast_maximum_fusion
  238.3 0.8 copy.24
  239.1 5.5 %all-to-all-start.2 = ((bf16[8,64,128]{2,1,0:T(8,128)(2,1)}), bf16[8,64,128]{2,1,0:T(8,128)(2,1)S(1)}, u32[]{:S(2)}, u32[]{:S(2)}) async-start(bf16[8,64,128]{2,1,0:T(8,128)(2,1)} %copy.24), calls=%async_computation.2 | async-start | bytes 262144 | tf_op jit(solution)/shard_map/all_to_all | solution.py:227
  244.7 5.0 %all-gather.5.cloned.1.call-done = bf16[1024,1024]{1,0:T(8,128)(2,1)} async-done(((bf16[128,1024]{1,0:T(8,128)(2,1)}), bf16[1024,1024]{1,0:T(8,128)(2,1)}) %all-gather.5.cloned.1.call-update) | async-done | bytes 2097168 | tf_op jit(solution)/shard_map/all_gather | solution.py:210
  249.7 1.4 all-to-all-done.2
  251.1 2.2 fusion.82
  253.8 19.2 %all_to_all.36 = bf16[8,64,1024]{2,1,0:T(8,128)(2,1)S(1)} all-to-all(bf16[8,64,1024]{2,1,0:T(8,128)(2,1)S(1)} %broadcast_in_dim.82), channel_id=1, replica_groups=mesh['req'=32,'tp'=8] {'tp'}, dimensions={0} | all-to-all | bytes 2097152 | tf_op jit(solution)/shard_map/all_to_all | solution.py:232
  273.0 4.6 %convolution_convert_fusion = bf16[512,1024]{1,0:T(8,128)(2,1)S(1)} fusion(bf16[512,1024]{1,0:T(8,128)(2,1)S(1)} %copy-done, bf16[512,1024]{1,0:T(8,128)(2,1)S(1)} %bitcast.70, bf16[1024,512]{1,0:T(8,128)(2,1)} %param.17, f32[512]{0:T(512)S(1)} %copy-done.8), kind=kOutput, calls=%fused_computation.7 | convolution fusion | flops 1091567616 | bytes 4196352 | tf_op jit(solution)/shard_map/dot_general | solution.py:239
  277.6 17.3 %all_to_all.37 = bf16[8,64,1024]{2,1,0:T(8,128)(2,1)S(1)} all-to-all(bf16[8,64,1024]{2,1,0:T(8,128)(2,1)S(1)} %bitcast.71), channel_id=1, replica_groups=mesh['req'=32,'tp'=8] {'tp'}, dimensions={0} | all-to-all | bytes 2097152 | tf_op jit(solution)/shard_map/all_to_all | solution.py:240
  295.6 0.8 add_convert_fusion
  (45 shorter events, 2.0 us)
Async XLA Ops:
  6.5 266.4 %copy-start = (bf16[512,1024]{1,0:T(8,128)(2,1)S(1)}, bf16[512,1024]{1,0:T(8,128)(2,1)}, u32[]{:S(2)}) copy-start(bf16[512,1024]{1,0:T(8,128)(2,1)} %param.19) | copy-start | bytes 3145732
  12.5 105.4 %all-to-all-start = ((bf16[32,512,128]{2,1,0:T(8,128)(2,1)}), bf16[32,512,128]{2,1,0:T(8,128)(2,1)}, u32[]{:S(2)}, u32[]{:S(2)}) async-start(bf16[32,512,128]{2,1,0:T(8,128)(2,1)} %get-tuple-element.20), calls=%async_computation | async-start | bytes 8388608 | tf_op jit(solution)/shard_map/all_to_all | solution.py:197
  118.0 8.5 %copy-start.1 = (bf16[1024,3,128]{2,0,1:T(8,128)(2,1)S(1)}, bf16[1024,3,128]{2,0,1:T(8,128)(2,1)}, u32[]{:S(2)}) copy-start(bf16[1024,3,128]{2,0,1:T(8,128)(2,1)} %param.15) | copy-start | bytes 2359300
  118.0 8.8 %copy-start.9 = (s32[32]{0:T(128)S(1)}, s32[32]{0:T(128)}, u32[]{:S(2)}) copy-start(s32[32]{0:T(128)} %param.26) | copy-start | bytes 388
  118.0 9.5 %copy-start.10 = (s32[32]{0:T(128)S(1)}, s32[32]{0:T(128)}, u32[]{:S(2)}) copy-start(s32[32]{0:T(128)} %param.27) | copy-start | bytes 388
  118.0 101.3 %all-to-all-start.1 = ((bf16[32,128,512]{2,1,0:T(8,128)(2,1)}), bf16[32,128,512]{2,1,0:T(8,128)(2,1)}, u32[]{:S(2)}, u32[]{:S(2)}) async-start(bf16[32,128,512]{2,1,0:T(8,128)(2,1)} %bitcast.68), calls=%async_computation.1 | async-start | bytes 8388608 | tf_op jit(solution)/shard_map/all_to_all | solution.py:199
  125.0 58.5 %all-gather.3.cloned.1.call-start = ((), (), s32[]{:S(2)}) async-start(), calls=%async_computation.5 | async-start | bytes 1179648 | tf_op jit(solution)/shard_map/all_gather | solution.py:201
  125.7 124.0 %all-gather.5.cloned.1.call-start = ((), (), s32[]{:S(2)}) async-start(), calls=%async_computation.6 | async-start | bytes 2359296 | tf_op jit(solution)/shard_map/all_gather | solution.py:210
  234.8 16.3 %copy-start.2 = (bf16[64,1024]{1,0:T(8,128)(2,1)S(1)}, bf16[64,1024]{1,0:T(8,128)(2,1)}, u32[]{:S(2)}) copy-start(bf16[64,1024]{1,0:T(8,128)(2,1)} %param.14) | copy-start | bytes 393220
  238.0 15.5 %copy-start.3 = (f32[1024]{0:T(1024)S(1)}, f32[1024]{0:T(1024)}, u32[]{:S(2)}) copy-start(f32[1024]{0:T(1024)} %param.22) | copy-start | bytes 12292
  238.0 15.5 %copy-start.4 = (f32[1024]{0:T(1024)S(1)}, f32[1024]{0:T(1024)}, u32[]{:S(2)}) copy-start(f32[1024]{0:T(1024)} %param.21) | copy-start | bytes 12292
  239.1 11.9 %all-to-all-start.2 = ((bf16[8,64,128]{2,1,0:T(8,128)(2,1)}), bf16[8,64,128]{2,1,0:T(8,128)(2,1)S(1)}, u32[]{:S(2)}, u32[]{:S(2)}) async-start(bf16[8,64,128]{2,1,0:T(8,128)(2,1)} %copy.24), calls=%async_computation.2 | async-start | bytes 262144 | tf_op jit(solution)/shard_map/all_to_all | solution.py:227
  253.3 19.7 %copy-start.8 = (f32[512]{0:T(512)S(1)}, f32[512]{0:T(512)}, u32[]{:S(2)}) copy-start(f32[512]{0:T(512)} %param.18) | copy-start | bytes 6148
  277.6 17.5 %copy-start.5 = (f32[1024]{0:T(1024)S(1)}, f32[1024]{0:T(1024)}, u32[]{:S(2)}) copy-start(f32[1024]{0:T(1024)} %param.20) | copy-start | bytes 12292
  277.6 18.0 %copy-start.6 = (f32[1024]{0:T(1024)S(1)}, f32[1024]{0:T(1024)}, u32[]{:S(2)}) copy-start(f32[1024]{0:T(1024)} %param.24) | copy-start | bytes 12292
  277.6 18.0 %copy-start.7 = (f32[1024]{0:T(1024)S(1)}, f32[1024]{0:T(1024)}, u32[]{:S(2)}) copy-start(f32[1024]{0:T(1024)} %param.23) | copy-start | bytes 12292
Sparse Core Ops, SparseCore 0:
  127.6 55.8 all-gather.2
  185.3 64.3 all-gather.4
where the time goes:
time: 306 us; the launch traced here: 303 us
  waiting for transfers between devices  153 us (50%)
  Pallas kernels  44.2 us (14%)
  blocking collectives  36.5 us (12%)
  starting transfers between devices  23.4 us (8%)
  local copies, waits for them, and re-layouts  17.7 us (6%)
  between operations  13.7 us (4%)
  matrix products  10 us (3%)
  other arithmetic  4.8 us (2%)
    all_to_all x1, waiting for transfers between devices, shards(): lax.all_to_all(kv_cache[0], 'req', split_axis=0, concat_axis=0, tiled=True)  88.2 us
    all_gather x1, waiting for transfers between devices, shards(): span_rows = lax.all_gather(tokens, 'tp', axis=0, tiled=True)  54.7 us
    pallas_call x1, Pallas kernels, block_weights(): pl.pallas_call(score_kernel, grid_spec=grid_spec, out_shape=[jax.ShapeDty...  28.7 us
    all_to_all x1, blocking collectives, shards(): lax.all_to_all(jnp.broadcast_to(normed[None], (n_tp,) + normed.shape), 't...  19.2 us
    all_to_all x1, blocking collectives, shards(): lax.all_to_all(partial.reshape((n_tp, -1) + partial.shape[1:]), 'tp', spl...  17.3 us
    pallas_call x1, Pallas kernels, cache_partials(): pl.pallas_call(blend_kernel, grid_spec=grid_spec, out_shape=[jax.ShapeDty...  15.5 us
    all_to_all x1, starting transfers between devices, shards(): lax.all_to_all(kv_cache[0], 'req', split_axis=0, concat_axis=0, tiled=True)  10.7 us
    unnamed x25, local copies, waits for them, and re-layouts  7.55 us
  transfers between devices with their start and end apart: 5, of which 5 were waited for; matrix products, arithmetic and copies ran while one was open for 6% of the time, Pallas kernels for 15%

commit v1 on v0

--- a/solution.py
+++ b/solution.py
@@ -224,14 +224,15 @@
         0,
     )
     attention = (blended / jnp.repeat(weight_sums, HEAD_DIM, axis=-1)).astype(jnp.bfloat16)
-    attention = lax.all_to_all(attention, "tp", split_axis=0, concat_axis=1, tiled=True)
+    n_tp = lax.axis_size("tp")
+    attention = lax.all_to_all(
+        jnp.broadcast_to(attention[None], (n_tp,) + attention.shape), "tp", split_axis=0, concat_axis=2, tiled=True
+    ).reshape(span, -1)
 
     projected = jnp.dot(attention, full_out, preferred_element_type=jnp.float32)
-    normed = layer_norm(tokens.astype(jnp.float32) + projected, ln1_gain, ln1_bias).astype(jnp.bfloat16)
-    n_tp = lax.axis_size("tp")
-    span_normed = lax.all_to_all(
-        jnp.broadcast_to(normed[None], (n_tp,) + normed.shape), "tp", split_axis=0, concat_axis=0, tiled=True
-    ).reshape(-1, normed.shape[1])
+    span_normed = layer_norm(span_rows.astype(jnp.float32) + projected, ln1_gain, ln1_bias).astype(jnp.bfloat16)
+    rows_here = tokens.shape[0]
+    normed = lax.dynamic_slice_in_dim(span_normed, lax.axis_index("tp") * rows_here, rows_here)
     hidden = jax.nn.gelu(
         jnp.dot(span_normed, w_up, preferred_element_type=jnp.float32) + b_up,
         approximate=False,

time: 306 us -> 301 us (0.984)
  blocking collectives: 36.5 us -> 0 us
  waiting for transfers between devices: 153 us -> 172 us
  Pallas kernels: 44.2 us -> 50.6 us
  starting transfers between devices: 23.4 us -> 27.7 us
    all_to_all x2 -> x0, blocking collectives: 36.5 us -> none  [the longest x1 19.2 us: shards(): lax.all_to_all(jnp.broadcast_to(normed[None], (n_tp,) + normed.shape), 't...]
    all_to_all x1 -> x2, waiting for transfers between devices: 1.38 us -> 19.7 us  [the longest x1 15.9 us: shards(): lax.all_to_all(partial.reshape((n_tp, -1) + partial.shape[1:]), 'tp', spl...]
    all_to_all x1 -> x2, starting transfers between devices: 5.54 us -> 9.84 us  [the longest x1 5.03 us: shards(): lax.all_to_all(jnp.broadcast_to(attention[None], (n_tp,) + attention.shap...]
    pallas_call x1, Pallas kernels: 28.7 us -> 32.9 us  [block_weights(): pl.pallas_call(score_kernel, grid_spec=grid_spec, out_shape=[jax.ShapeDty...]
    unnamed x25 -> x27, local copies, waits for them, and re-layouts: 7.55 us -> 8.29 us
  transfers between devices with their start and end apart: 5 -> 6, of which waited for: 5 -> 5; matrix products, arithmetic and copies ran while one was open for 6% -> 6% of each run, Pallas kernels for 15% -> 17%
where the time goes in v1:
time: 301 us; the launch traced here: 297 us
  waiting for transfers between devices  172 us (57%)
  Pallas kernels  50.6 us (17%)
  starting transfers between devices  27.7 us (9%)
  local copies, waits for them, and re-layouts  18.3 us (6%)
  between operations  13.6 us (5%)
  matrix products  10.5 us (3%)
  other arithmetic  5.07 us (2%)
    all_to_all x1, waiting for transfers between devices, shards(): lax.all_to_all(kv_cache[0], 'req', split_axis=0, concat_axis=0, tiled=True)  88.2 us
    all_gather x1, waiting for transfers between devices, shards(): span_rows = lax.all_gather(tokens, 'tp', axis=0, tiled=True)  54.7 us
    pallas_call x1, Pallas kernels, block_weights(): pl.pallas_call(score_kernel, grid_spec=grid_spec, out_shape=[jax.ShapeDty...  32.9 us
    pallas_call x1, Pallas kernels, cache_partials(): pl.pallas_call(blend_kernel, grid_spec=grid_spec, out_shape=[jax.ShapeDty...  17.7 us
    all_to_all x1, waiting for transfers between devices, shards(): lax.all_to_all(partial.reshape((n_tp, -1) + partial.shape[1:]), 'tp', spl...  15.9 us
    all_to_all x1, starting transfers between devices, shards(): lax.all_to_all(kv_cache[0], 'req', split_axis=0, concat_axis=0, tiled=True)  10.7 us
    unnamed x27, local copies, waits for them, and re-layouts  8.29 us
    all_gather x1, waiting for transfers between devices, shards(): full_out = lax.all_gather(w_out, 'tp', axis=0, tiled=True)  7.7 us
  transfers between devices with their start and end apart: 6, of which 5 were waited for; matrix products, arithmetic and copies ran while one was open for 6% of the time, Pallas kernels for 17%

profile of v1, /device:TPU:80, one launch (start us, length us, event | category | flops | bytes accessed | tf_op | source)
XLA Modules:
  0.0 297.4 jit_solution(3058593799211734619)
XLA Ops:
  6.5 6.0 %fusion.78 = (bf16[1,32,512,128]{3,2,1,0:T(8,128)(2,1)}, bf16[32,512,128]{2,1,0:T(8,128)(2,1)}) fusion(bf16[2,32,512,128]{3,2,1,0:T(8,128)(2,1)} %param.25), kind=kLoop, calls=%fused_computation.126 | loop fusion | bytes 16777216 | tf_op jit(solution)/shard_map/slice | solution.py:198
  12.5 10.7 %all-to-all-start = ((bf16[32,512,128]{2,1,0:T(8,128)(2,1)}), bf16[32,512,128]{2,1,0:T(8,128)(2,1)}, u32[]{:S(2)}, u32[]{:S(2)}) async-start(bf16[32,512,128]{2,1,0:T(8,128)(2,1)} %get-tuple-element.20), calls=%async_computation | async-start | bytes 8388608 | tf_op jit(solution)/shard_map/all_to_all | solution.py:197
  23.3 6.5 %copy.22 = bf16[1,32,512,128]{2,3,1,0:T(8,128)(2,1)} copy(bf16[1,32,512,128]{3,2,1,0:T(8,128)(2,1)} %get-tuple-element.19) | data formatting | bytes 8388608
  29.8 88.2 %all-to-all-done.k_ref = bf16[32,512,128]{2,1,0:T(8,128)(2,1)} async-done(((bf16[32,512,128]{2,1,0:T(8,128)(2,1)}), bf16[32,512,128]{2,1,0:T(8,128)(2,1)}, u32[]{:S(2)}, u32[]{:S(2)}) %all-to-all-start) | async-done | bytes 4194336 | tf_op jit(solution)/shard_map/all_to_all | solution.py:197
  118.0 7.0 %all-to-all-start.1 = ((bf16[32,128,512]{2,1,0:T(8,128)(2,1)}), bf16[32,128,512]{2,1,0:T(8,128)(2,1)}, u32[]{:S(2)}, u32[]{:S(2)}) async-start(bf16[32,128,512]{2,1,0:T(8,128)(2,1)} %bitcast.62), calls=%async_computation.1 | async-start | bytes 8388608 | tf_op jit(solution)/shard_map/all_to_all | solution.py:199
  125.1 0.7 all-gather.3.cloned.1.call-update
  125.8 0.7 all-gather.5.cloned.1.call-update
  126.8 0.6 dynamic_slice.10.count_ref
  127.4 0.6 dynamic_slice.9
  128.0 0.6 iota_compare_fusion.1
  128.8 54.7 %all-gather.3.cloned.1.call-done = bf16[512,1024]{1,0:T(8,128)(2,1)} async-done(((bf16[64,1024]{1,0:T(8,128)(2,1)}), bf16[512,1024]{1,0:T(8,128)(2,1)}) %all-gather.3.cloned.1.call-update) | async-done | bytes 1048592 | tf_op jit(solution)/shard_map/all_gather | solution.py:201
  183.5 1.8 convolution_convert_fusion.1
  185.4 0.6 fusion
  186.0 0.8 convolution_bitcast_fusion
  186.8 0.8 broadcast_select_fusion.qt_ref
  187.6 0.6 convert_reduce_fusion.1
  188.2 32.9 %shard_map.136 = (bf16[32,2,512,512]{3,2,1,0:T(8,128)(2,1)}, f32[32,2,1,512]{3,2,1,0:T(1,128)}) custom-call(s32[1]{0:T(128)} %dynamic_slice.10.count_ref, bf16[2,128,512]{2,1,0:T(8,128)(2,1)} %broadcast_select_fusion.qt_ref, bf16[32,512,128]{2,1,0:T(8,128)(2,1)} %all-to-all-done.k_ref), custom_call_target="tpu_custom_call" | custom-call | flops 4294967296 | bytes 37748736 | tf_op jit(solution)/shard_map/pallas_call | solution.py:124
  221.1 17.7 %shard_map.137 = (f32[2,128,512]{2,1,0:T(8,128)}, f32[2,1,512]{2,1,0:T(1,128)}) custom-call(s32[1]{0:T(128)} %dynamic_slice.10.count_ref, bf16[32,2,512,512]{3,2,1,0:T(8,128)(2,1)} %get-tuple-element.12.w_ref, f32[32,2,1,512]{3,2,1,0:T(1,128)} %get-tuple-element.13.block_peak_ref, bf16[32,128,512]{2,1,0:T(8,128)(2,1)} %all-to-all-done.1.vt_ref), custom_call_target="tpu_custom_call" | custom-call | flops 4294967296 | bytes 38273024 | tf_op jit(solution)/shard_map/pallas_call | solution.py:157
  238.8 0.7 copy.25
  239.5 0.7 slice_bitcast_fusion.4
  240.2 1.0 slice_bitcast_fusion.2
  241.2 0.7 bitcast_maximum_fusion
  242.1 1.1 broadcast_in_dim.82
  243.1 5.0 %all-to-all-start.2 = ((bf16[8,512,128]{1,2,0:T(8,128)(2,1)}), bf16[8,512,128]{1,2,0:T(8,128)(2,1)S(1)}, u32[]{:S(2)}, u32[]{:S(2)}) async-start(bf16[8,512,128]{1,2,0:T(8,128)(2,1)} %broadcast_in_dim.82), calls=%async_computation.2 | async-start | bytes 2097152 | tf_op jit(solution)/shard_map/all_to_all | solution.py:228
  248.1 7.7 %all-gather.5.cloned.1.call-done = bf16[1024,1024]{1,0:T(8,128)(2,1)} async-done(((bf16[128,1024]{1,0:T(8,128)(2,1)}), bf16[1024,1024]{1,0:T(8,128)(2,1)}) %all-gather.5.cloned.1.call-update) | async-done | bytes 2097168 | tf_op jit(solution)/shard_map/all_gather | solution.py:210
  255.8 3.7 %all-to-all-done.2 = bf16[8,512,128]{1,2,0:T(8,128)(2,1)S(1)} async-done(((bf16[8,512,128]{1,2,0:T(8,128)(2,1)}), bf16[8,512,128]{1,2,0:T(8,128)(2,1)S(1)}, u32[]{:S(2)}, u32[]{:S(2)}) %all-to-all-start.2) | async-done | bytes 1048608 | tf_op jit(solution)/shard_map/all_to_all | solution.py:228
  259.6 2.9 fusion.80
  263.7 0.5 copy-done.8
  264.1 4.4 %convolution_convert_fusion = bf16[512,1024]{1,0:T(8,128)(2,1)} fusion(bf16[512,1024]{1,0:T(8,128)(2,1)S(1)} %copy-done, bf16[512,1024]{1,0:T(8,128)(2,1)S(1)} %add_convert_fusion, bf16[1024,512]{1,0:T(8,128)(2,1)S(1)} %copy-done.8, f32[512]{0:T(512)S(1)} %copy-done.9), kind=kOutput, calls=%fused_computation.10 | convolution fusion | flops 1091567616 | bytes 4196352 | tf_op jit(solution)/shard_map/dot_general | solution.py:240
  268.5 4.8 %all-to-all-start.3 = ((bf16[8,64,1024]{2,1,0:T(8,128)(2,1)}), bf16[8,64,1024]{2,1,0:T(8,128)(2,1)S(1)}, u32[]{:S(2)}, u32[]{:S(2)}) async-start(bf16[8,64,1024]{2,1,0:T(8,128)(2,1)} %bitcast.65), calls=%async_computation.3 | async-start | bytes 2097152 | tf_op jit(solution)/shard_map/all_to_all | solution.py:241
  273.3 15.9 %all-to-all-done.3 = bf16[8,64,1024]{2,1,0:T(8,128)(2,1)S(1)} async-done(((bf16[8,64,1024]{2,1,0:T(8,128)(2,1)}), bf16[8,64,1024]{2,1,0:T(8,128)(2,1)S(1)}, u32[]{:S(2)}, u32[]{:S(2)}) %all-to-all-start.3) | async-done | bytes 1048608 | tf_op jit(solution)/shard_map/all_to_all | solution.py:241
  289.8 0.8 add_convert_fusion.1
  (45 shorter events, 2.3 us)
Async XLA Ops:
  6.5 257.1 %copy-start = (bf16[512,1024]{1,0:T(8,128)(2,1)S(1)}, bf16[512,1024]{1,0:T(8,128)(2,1)}, u32[]{:S(2)}) copy-start(bf16[512,1024]{1,0:T(8,128)(2,1)} %param.19) | copy-start | bytes 3145732
  12.5 105.4 %all-to-all-start = ((bf16[32,512,128]{2,1,0:T(8,128)(2,1)}), bf16[32,512,128]{2,1,0:T(8,128)(2,1)}, u32[]{:S(2)}, u32[]{:S(2)}) async-start(bf16[32,512,128]{2,1,0:T(8,128)(2,1)} %get-tuple-element.20), calls=%async_computation | async-start | bytes 8388608 | tf_op jit(solution)/shard_map/all_to_all | solution.py:197
  118.0 8.5 %copy-start.2 = (bf16[1024,3,128]{2,0,1:T(8,128)(2,1)S(1)}, bf16[1024,3,128]{2,0,1:T(8,128)(2,1)}, u32[]{:S(2)}) copy-start(bf16[1024,3,128]{2,0,1:T(8,128)(2,1)} %param.15) | copy-start | bytes 2359300
  118.0 8.8 %copy-start.10 = (s32[32]{0:T(128)S(1)}, s32[32]{0:T(128)}, u32[]{:S(2)}) copy-start(s32[32]{0:T(128)} %param.26) | copy-start | bytes 388
  118.0 9.4 %copy-start.11 = (s32[32]{0:T(128)S(1)}, s32[32]{0:T(128)}, u32[]{:S(2)}) copy-start(s32[32]{0:T(128)} %param.27) | copy-start | bytes 388
  118.0 103.1 %all-to-all-start.1 = ((bf16[32,128,512]{2,1,0:T(8,128)(2,1)}), bf16[32,128,512]{2,1,0:T(8,128)(2,1)}, u32[]{:S(2)}, u32[]{:S(2)}) async-start(bf16[32,128,512]{2,1,0:T(8,128)(2,1)} %bitcast.62), calls=%async_computation.1 | async-start | bytes 8388608 | tf_op jit(solution)/shard_map/all_to_all | solution.py:199
  125.0 58.5 %all-gather.3.cloned.1.call-start = ((), (), s32[]{:S(2)}) async-start(), calls=%async_computation.4 | async-start | bytes 1179648 | tf_op jit(solution)/shard_map/all_gather | solution.py:201
  125.7 130.1 %all-gather.5.cloned.1.call-start = ((), (), s32[]{:S(2)}) async-start(), calls=%async_computation.5 | async-start | bytes 2359296 | tf_op jit(solution)/shard_map/all_gather | solution.py:210
  242.0 17.6 %copy-start.1 = (bf16[512,1024]{1,0:T(8,128)(2,1)S(1)}, bf16[512,1024]{1,0:T(8,128)(2,1)}, u32[]{:S(2)}) copy-start(bf16[512,1024]{1,0:T(8,128)(2,1)} %all-gather.3.cloned.1.call-done) | copy-start | bytes 3145732
  243.1 16.5 %all-to-all-start.2 = ((bf16[8,512,128]{1,2,0:T(8,128)(2,1)}), bf16[8,512,128]{1,2,0:T(8,128)(2,1)S(1)}, u32[]{:S(2)}, u32[]{:S(2)}) async-start(bf16[8,512,128]{1,2,0:T(8,128)(2,1)} %broadcast_in_dim.82), calls=%async_computation.2 | async-start | bytes 2097152 | tf_op jit(solution)/shard_map/all_to_all | solution.py:228
  262.5 0.7 copy-start.4
  262.5 0.7 copy-start.5
  262.9 1.2 copy-start.8
  262.9 1.2 copy-start.9
  268.5 20.9 %copy-start.3 = (f32[1024]{0:T(1024)S(1)}, f32[1024]{0:T(1024)}, u32[]{:S(2)}) copy-start(f32[1024]{0:T(1024)} %param.20) | copy-start | bytes 12292
  268.5 21.3 %copy-start.6 = (f32[1024]{0:T(1024)S(1)}, f32[1024]{0:T(1024)}, u32[]{:S(2)}) copy-start(f32[1024]{0:T(1024)} %param.24) | copy-start | bytes 12292
  268.5 21.3 %copy-start.7 = (f32[1024]{0:T(1024)S(1)}, f32[1024]{0:T(1024)}, u32[]{:S(2)}) copy-start(f32[1024]{0:T(1024)} %param.23) | copy-start | bytes 12292
  268.5 20.8 %all-to-all-start.3 = ((bf16[8,64,1024]{2,1,0:T(8,128)(2,1)}), bf16[8,64,1024]{2,1,0:T(8,128)(2,1)S(1)}, u32[]{:S(2)}, u32[]{:S(2)}) async-start(bf16[8,64,1024]{2,1,0:T(8,128)(2,1)} %bitcast.65), calls=%async_computation.3 | async-start | bytes 2097152 | tf_op jit(solution)/shard_map/all_to_all | solution.py:241
Sparse Core Ops, SparseCore 0:
  127.6 55.8 all-gather.2
  185.3 70.4 all-gather.4

commit v2 on v1

--- a/solution.py
+++ b/solution.py
@@ -6,7 +6,7 @@
 from jax.sharding import PartitionSpec as P
 
 HEAD_DIM = 64
-BLEND_STEP = 4
+BLEND_STEP = 8
 
 masked_score = -1e30
 

time: 301 us -> 301 us (level)
  Pallas kernels: 50.6 us -> 38.8 us
  waiting for transfers between devices: 172 us -> 183 us
    all_gather x1, waiting for transfers between devices: 7.7 us -> 16.3 us  [shards(): full_out = lax.all_gather(w_out, 'tp', axis=0, tiled=True)]
    pallas_call x1, Pallas kernels: 32.9 us -> 25.3 us  [block_weights(): pl.pallas_call(score_kernel, grid_spec=grid_spec, out_shape=[jax.ShapeDty...]
    all_to_all x1, waiting for transfers between devices: 0.01 us -> 5.72 us  [shards(): lax.all_to_all(value_rows, 'req', split_axis=0, concat_axis=0, tiled=True)]
    pallas_call x1, Pallas kernels: 17.7 us -> 13.5 us  [cache_partials(): pl.pallas_call(blend_kernel, grid_spec=grid_spec, out_shape=[jax.ShapeDty...]
    all_to_all x1, waiting for transfers between devices: 3.74 us -> 0.62 us  [shards(): lax.all_to_all(jnp.broadcast_to(attention[None], (n_tp,) + attention.shap...]
  transfers between devices with their start and end apart: 6 -> 6, of which waited for: 5 -> 6; matrix products, arithmetic and copies ran while one was open for 6% -> 6% of each run, Pallas kernels for 17% -> 13%
where the time goes in v2:
time: 301 us; the launch traced here: 297 us
  waiting for transfers between devices  183 us (61%)
  Pallas kernels  38.8 us (13%)
  starting transfers between devices  28.6 us (10%)
  local copies, waits for them, and re-layouts  18.3 us (6%)
  between operations  13.6 us (5%)
  matrix products  10.5 us (3%)
  other arithmetic  5.07 us (2%)
    all_to_all x1, waiting for transfers between devices, shards(): lax.all_to_all(kv_cache[0], 'req', split_axis=0, concat_axis=0, tiled=True)  88.2 us
    all_gather x1, waiting for transfers between devices, shards(): span_rows = lax.all_gather(tokens, 'tp', axis=0, tiled=True)  54.7 us
    pallas_call x1, Pallas kernels, block_weights(): pl.pallas_call(score_kernel, grid_spec=grid_spec, out_shape=[jax.ShapeDty...  25.3 us
    all_gather x1, waiting for transfers between devices, shards(): full_out = lax.all_gather(w_out, 'tp', axis=0, tiled=True)  16.3 us
    all_to_all x1, waiting for transfers between devices, shards(): lax.all_to_all(partial.reshape((n_tp, -1) + partial.shape[1:]), 'tp', spl...  15.6 us
    pallas_call x1, Pallas kernels, cache_partials(): pl.pallas_call(blend_kernel, grid_spec=grid_spec, out_shape=[jax.ShapeDty...  13.5 us
    all_to_all x1, starting transfers between devices, shards(): lax.all_to_all(kv_cache[0], 'req', split_axis=0, concat_axis=0, tiled=True)  10.7 us
    unnamed x27, local copies, waits for them, and re-layouts  8.29 us
  transfers between devices with their start and end apart: 6, of which 6 were waited for; matrix products, arithmetic and copies ran while one was open for 6% of the time, Pallas kernels for 13%

profile of v2, /device:TPU:80, one launch (start us, length us, event | category | flops | bytes accessed | tf_op | source)
XLA Modules:
  0.0 297.5 jit_solution(5256141530860488555)
XLA Ops:
  6.5 6.0 %fusion.78 = (bf16[1,32,512,128]{3,2,1,0:T(8,128)(2,1)}, bf16[32,512,128]{2,1,0:T(8,128)(2,1)}) fusion(bf16[2,32,512,128]{3,2,1,0:T(8,128)(2,1)} %param.25), kind=kLoop, calls=%fused_computation.126 | loop fusion | bytes 16777216 | tf_op jit(solution)/shard_map/slice | solution.py:198
  12.5 10.7 %all-to-all-start = ((bf16[32,512,128]{2,1,0:T(8,128)(2,1)}), bf16[32,512,128]{2,1,0:T(8,128)(2,1)}, u32[]{:S(2)}, u32[]{:S(2)}) async-start(bf16[32,512,128]{2,1,0:T(8,128)(2,1)} %get-tuple-element.20), calls=%async_computation | async-start | bytes 8388608 | tf_op jit(solution)/shard_map/all_to_all | solution.py:197
  23.3 6.5 %copy.22 = bf16[1,32,512,128]{2,3,1,0:T(8,128)(2,1)} copy(bf16[1,32,512,128]{3,2,1,0:T(8,128)(2,1)} %get-tuple-element.19) | data formatting | bytes 8388608
  29.8 88.2 %all-to-all-done.k_ref = bf16[32,512,128]{2,1,0:T(8,128)(2,1)} async-done(((bf16[32,512,128]{2,1,0:T(8,128)(2,1)}), bf16[32,512,128]{2,1,0:T(8,128)(2,1)}, u32[]{:S(2)}, u32[]{:S(2)}) %all-to-all-start) | async-done | bytes 4194336 | tf_op jit(solution)/shard_map/all_to_all | solution.py:197
  118.0 7.0 %all-to-all-start.1 = ((bf16[32,128,512]{2,1,0:T(8,128)(2,1)}), bf16[32,128,512]{2,1,0:T(8,128)(2,1)}, u32[]{:S(2)}, u32[]{:S(2)}) async-start(bf16[32,128,512]{2,1,0:T(8,128)(2,1)} %bitcast.62), calls=%async_computation.1 | async-start | bytes 8388608 | tf_op jit(solution)/shard_map/all_to_all | solution.py:199
  125.1 0.7 all-gather.3.cloned.1.call-update
  125.8 0.7 all-gather.5.cloned.1.call-update
  126.8 0.6 dynamic_slice.10.count_ref
  127.4 0.6 dynamic_slice.9
  128.0 0.6 iota_compare_fusion.1
  128.8 54.7 %all-gather.3.cloned.1.call-done = bf16[512,1024]{1,0:T(8,128)(2,1)} async-done(((bf16[64,1024]{1,0:T(8,128)(2,1)}), bf16[512,1024]{1,0:T(8,128)(2,1)}) %all-gather.3.cloned.1.call-update) | async-done | bytes 1048592 | tf_op jit(solution)/shard_map/all_gather | solution.py:201
  183.5 1.8 convolution_convert_fusion.1
  185.4 0.6 fusion
  186.0 0.8 convolution_bitcast_fusion
  186.8 0.8 broadcast_select_fusion.qt_ref
  187.6 0.6 convert_reduce_fusion.1
  188.2 25.3 %shard_map.136 = (bf16[32,2,512,512]{3,2,1,0:T(8,128)(2,1)}, f32[32,2,1,512]{3,2,1,0:T(1,128)}) custom-call(s32[1]{0:T(128)} %dynamic_slice.10.count_ref, bf16[2,128,512]{2,1,0:T(8,128)(2,1)} %broadcast_select_fusion.qt_ref, bf16[32,512,128]{2,1,0:T(8,128)(2,1)} %all-to-all-done.k_ref), custom_call_target="tpu_custom_call" | custom-call | flops 4294967296 | bytes 37748736 | tf_op jit(solution)/shard_map/pallas_call | solution.py:124
  213.5 5.7 %all-to-all-done.1.vt_ref = bf16[32,128,512]{2,1,0:T(8,128)(2,1)} async-done(((bf16[32,128,512]{2,1,0:T(8,128)(2,1)}), bf16[32,128,512]{2,1,0:T(8,128)(2,1)}, u32[]{:S(2)}, u32[]{:S(2)}) %all-to-all-start.1) | async-done | bytes 4194336 | tf_op jit(solution)/shard_map/all_to_all | solution.py:199
  219.3 13.5 %shard_map.137 = (f32[2,128,512]{2,1,0:T(8,128)}, f32[2,1,512]{2,1,0:T(1,128)}) custom-call(s32[1]{0:T(128)} %dynamic_slice.10.count_ref, bf16[32,2,512,512]{3,2,1,0:T(8,128)(2,1)} %get-tuple-element.12.w_ref, f32[32,2,1,512]{3,2,1,0:T(1,128)} %get-tuple-element.13.block_peak_ref, bf16[32,128,512]{2,1,0:T(8,128)(2,1)} %all-to-all-done.1.vt_ref), custom_call_target="tpu_custom_call" | custom-call | flops 4294967296 | bytes 38273024 | tf_op jit(solution)/shard_map/pallas_call | solution.py:157
  232.8 0.7 copy.25
  233.5 0.7 slice_bitcast_fusion.4
  234.2 1.0 slice_bitcast_fusion.2
  235.2 0.7 bitcast_maximum_fusion
  236.0 1.1 broadcast_in_dim.82
  237.1 5.5 %all-to-all-start.2 = ((bf16[8,512,128]{1,2,0:T(8,128)(2,1)}), bf16[8,512,128]{1,2,0:T(8,128)(2,1)S(1)}, u32[]{:S(2)}, u32[]{:S(2)}) async-start(bf16[8,512,128]{1,2,0:T(8,128)(2,1)} %broadcast_in_dim.82), calls=%async_computation.2 | async-start | bytes 2097152 | tf_op jit(solution)/shard_map/all_to_all | solution.py:228
  242.6 16.3 %all-gather.5.cloned.1.call-done = bf16[1024,1024]{1,0:T(8,128)(2,1)} async-done(((bf16[128,1024]{1,0:T(8,128)(2,1)}), bf16[1024,1024]{1,0:T(8,128)(2,1)}) %all-gather.5.cloned.1.call-update) | async-done | bytes 2097168 | tf_op jit(solution)/shard_map/all_gather | solution.py:210
  258.9 0.6 all-to-all-done.2
  259.6 2.9 fusion.80
  264.1 4.4 %convolution_convert_fusion = bf16[512,1024]{1,0:T(8,128)(2,1)} fusion(bf16[512,1024]{1,0:T(8,128)(2,1)S(1)} %copy-done, bf16[512,1024]{1,0:T(8,128)(2,1)S(1)} %add_convert_fusion, bf16[1024,512]{1,0:T(8,128)(2,1)S(1)} %copy-done.8, f32[512]{0:T(512)S(1)} %copy-done.9), kind=kOutput, calls=%fused_computation.10 | convolution fusion | flops 1091567616 | bytes 4196352 | tf_op jit(solution)/shard_map/dot_general | solution.py:240
  268.5 5.2 %all-to-all-start.3 = ((bf16[8,64,1024]{2,1,0:T(8,128)(2,1)}), bf16[8,64,1024]{2,1,0:T(8,128)(2,1)S(1)}, u32[]{:S(2)}, u32[]{:S(2)}) async-start(bf16[8,64,1024]{2,1,0:T(8,128)(2,1)} %bitcast.65), calls=%async_computation.3 | async-start | bytes 2097152 | tf_op jit(solution)/shard_map/all_to_all | solution.py:241
  273.7 15.6 %all-to-all-done.3 = bf16[8,64,1024]{2,1,0:T(8,128)(2,1)S(1)} async-done(((bf16[8,64,1024]{2,1,0:T(8,128)(2,1)}), bf16[8,64,1024]{2,1,0:T(8,128)(2,1)S(1)}, u32[]{:S(2)}, u32[]{:S(2)}) %all-to-all-start.3) | async-done | bytes 1048608 | tf_op jit(solution)/shard_map/all_to_all | solution.py:241
  289.9 0.8 add_convert_fusion.1
  (45 shorter events, 2.8 us)
Async XLA Ops:
  6.5 257.1 %copy-start = (bf16[512,1024]{1,0:T(8,128)(2,1)S(1)}, bf16[512,1024]{1,0:T(8,128)(2,1)}, u32[]{:S(2)}) copy-start(bf16[512,1024]{1,0:T(8,128)(2,1)} %param.19) | copy-start | bytes 3145732
  12.5 105.4 %all-to-all-start = ((bf16[32,512,128]{2,1,0:T(8,128)(2,1)}), bf16[32,512,128]{2,1,0:T(8,128)(2,1)}, u32[]{:S(2)}, u32[]{:S(2)}) async-start(bf16[32,512,128]{2,1,0:T(8,128)(2,1)} %get-tuple-element.20), calls=%async_computation | async-start | bytes 8388608 | tf_op jit(solution)/shard_map/all_to_all | solution.py:197
  118.0 8.5 %copy-start.2 = (bf16[1024,3,128]{2,0,1:T(8,128)(2,1)S(1)}, bf16[1024,3,128]{2,0,1:T(8,128)(2,1)}, u32[]{:S(2)}) copy-start(bf16[1024,3,128]{2,0,1:T(8,128)(2,1)} %param.15) | copy-start | bytes 2359300
  118.0 8.8 %copy-start.10 = (s32[32]{0:T(128)S(1)}, s32[32]{0:T(128)}, u32[]{:S(2)}) copy-start(s32[32]{0:T(128)} %param.26) | copy-start | bytes 388
  118.0 9.4 %copy-start.11 = (s32[32]{0:T(128)S(1)}, s32[32]{0:T(128)}, u32[]{:S(2)}) copy-start(s32[32]{0:T(128)} %param.27) | copy-start | bytes 388
  118.0 101.3 %all-to-all-start.1 = ((bf16[32,128,512]{2,1,0:T(8,128)(2,1)}), bf16[32,128,512]{2,1,0:T(8,128)(2,1)}, u32[]{:S(2)}, u32[]{:S(2)}) async-start(bf16[32,128,512]{2,1,0:T(8,128)(2,1)} %bitcast.62), calls=%async_computation.1 | async-start | bytes 8388608 | tf_op jit(solution)/shard_map/all_to_all | solution.py:199
  125.0 58.5 %all-gather.3.cloned.1.call-start = ((), (), s32[]{:S(2)}) async-start(), calls=%async_computation.4 | async-start | bytes 1179648 | tf_op jit(solution)/shard_map/all_gather | solution.py:201
  125.7 133.2 %all-gather.5.cloned.1.call-start = ((), (), s32[]{:S(2)}) async-start(), calls=%async_computation.5 | async-start | bytes 2359296 | tf_op jit(solution)/shard_map/all_gather | solution.py:210
  235.9 23.6 %copy-start.1 = (bf16[512,1024]{1,0:T(8,128)(2,1)S(1)}, bf16[512,1024]{1,0:T(8,128)(2,1)}, u32[]{:S(2)}) copy-start(bf16[512,1024]{1,0:T(8,128)(2,1)} %all-gather.3.cloned.1.call-done) | copy-start | bytes 3145732
  237.1 22.5 %all-to-all-start.2 = ((bf16[8,512,128]{1,2,0:T(8,128)(2,1)}), bf16[8,512,128]{1,2,0:T(8,128)(2,1)S(1)}, u32[]{:S(2)}, u32[]{:S(2)}) async-start(bf16[8,512,128]{1,2,0:T(8,128)(2,1)} %broadcast_in_dim.82), calls=%async_computation.2 | async-start | bytes 2097152 | tf_op jit(solution)/shard_map/all_to_all | solution.py:228
  262.5 0.7 copy-start.4
  262.5 0.7 copy-start.5
  262.9 1.2 copy-start.8
  262.9 1.2 copy-start.9
  268.5 21.0 %copy-start.3 = (f32[1024]{0:T(1024)S(1)}, f32[1024]{0:T(1024)}, u32[]{:S(2)}) copy-start(f32[1024]{0:T(1024)} %param.20) | copy-start | bytes 12292
  268.5 21.4 %copy-start.6 = (f32[1024]{0:T(1024)S(1)}, f32[1024]{0:T(1024)}, u32[]{:S(2)}) copy-start(f32[1024]{0:T(1024)} %param.24) | copy-start | bytes 12292
  268.5 21.4 %copy-start.7 = (f32[1024]{0:T(1024)S(1)}, f32[1024]{0:T(1024)}, u32[]{:S(2)}) copy-start(f32[1024]{0:T(1024)} %param.23) | copy-start | bytes 12292
  268.5 20.8 %all-to-all-start.3 = ((bf16[8,64,1024]{2,1,0:T(8,128)(2,1)}), bf16[8,64,1024]{2,1,0:T(8,128)(2,1)S(1)}, u32[]{:S(2)}, u32[]{:S(2)}) async-start(bf16[8,64,1024]{2,1,0:T(8,128)(2,1)} %bitcast.65), calls=%async_computation.3 | async-start | bytes 2097152 | tf_op jit(solution)/shard_map/all_to_all | solution.py:241
Sparse Core Ops, SparseCore 0:
  127.6 55.8 all-gather.2
  185.3 73.5 all-gather.4
